TPU v7x, 32 devices: a whole 2x2x4 slice. The times are simulated.
32 devices in a mesh: cap: 4 (over z), lat: 4 (over x, core), rad: 2 (over y).
Axes of the slice: x: 2, y: 2, z: 4, core: 2. Of those that a mesh axis runs over, the one named last changes fastest.
Arguments:
- adjoint_temp: float32 [64, 128, 1024], P('rad', 'cap', 'lat'), may hold values from -6 to 6
- velocity: bfloat16 [2, 64, 128, 1024], P(None, 'rad', 'cap', 'lat'), may hold values from -6 to 6
- visc_flow: bfloat16 [64, 128, 1024], P('rad', 'cap', 'lat'), may hold values from 0.099609375 to 1
- visc_yield: bfloat16 [64, 128, 1024], P('rad', 'cap', 'lat'), may hold values from 0.049804688 to 1
- yield_mask: int32 [64, 128, 1024], P('rad', 'cap', 'lat'), may hold values 0 or 1
- radial_inverse: float32 [64, 64], replicated
- marker_rows: bfloat16 [64, 32768], P('rad', ('cap', 'lat')), may hold values from -6 to 6
- recv_cells: int32 [32768], P(('cap', 'lat')), may hold values from 0 to 8191
- recv_counts: int32 [64], P(('cap', 'lat')), may hold values from 64 to 512, as said below
Outputs:
- adjoint_prev: float32 [64, 128, 1024], P(None, ('cap', 'rad'), 'lat')
Inputs may be any that keep to these rules, and one draw needn't show every extreme that they name: `recv_counts`: some bucket holds exactly 512 live slots and some exactly 64 in every draw.
All inputs are finite; a program needn't handle non-finite values. No bound on the sum of `yield_mask` on one device may be relied on, other than what follows from the above.
Results may differ from a plain program's by a relative error of at most 0.0003.
Values may be sent and summed in bfloat16 or wider, within the bound.
No kernel may reach another device: no remote copies, remote signals or barrier semaphores. Data moves between devices by JAX's collectives and lax.ppermute only.
A program may use at most 64 MiB of HBM per device.

v0:
```python
import math
import jax
import jax.numpy as jnp
from jax import lax
from jax.sharding import PartitionSpec as P

PICARD = 3
relax_coef = 0.25
advect_coef = 0.1


def extended(x, sides, width):
    for axis, dim in sides:
        devices, length = (lax.axis_size(axis), x.shape[dim])
        up = [(i, (i + 1) % devices) for i in range(devices - 1)]
        down = [(j, i) for i, j in up]
        last = lax.slice_in_dim(x, length - width, length, axis=dim)
        first = lax.slice_in_dim(x, 0, width, axis=dim)
        before = lax.ppermute(last, axis, up)
        after = lax.ppermute(first, axis, down)
        x = jnp.concatenate([before, x, after], axis=dim)
    return x


def viscous(w_pad, eta_pad, w_mid, eta_mid):
    total = jnp.zeros_like(w_mid)
    for neigh_w, neigh_e in (
        (w_pad[:, 2:, 1:-1], eta_pad[:, 2:, 1:-1]),
        (w_pad[:, :-2, 1:-1], eta_pad[:, :-2, 1:-1]),
        (w_pad[:, 1:-1, 2:], eta_pad[:, 1:-1, 2:]),
        (w_pad[:, 1:-1, :-2], eta_pad[:, 1:-1, :-2]),
    ):
        total = total + 0.5 * (eta_mid + neigh_e) * (neigh_w - w_mid)
    return total


def per_device(
    adjoint_temp,
    velocity,
    visc_flow,
    visc_yield,
    yield_mask,
    radial_inverse,
    marker_rows,
    recv_cells,
    recv_counts,
):
    layers, first_len, second_len = adjoint_temp.shape
    flow = visc_flow.astype(jnp.float32)
    plast = visc_yield.astype(jnp.float32)
    eta = jnp.where(yield_mask == 1, flow * plast / (flow + plast), flow)
    iterate = adjoint_temp
    lam_pad = None
    for sweep in range(PICARD):
        padded = extended(jnp.stack([iterate, eta]), (("cap", 2), ("lat", 3)), 1)
        if sweep == 0:
            lam_pad = padded[0]
        iterate = adjoint_temp + relax_coef * viscous(padded[0], padded[1], iterate, eta)
    advect = velocity[0] * (lam_pad[:, 2:, 1:-1] - lam_pad[:, :-2, 1:-1]) + velocity[1] * (
        lam_pad[:, 1:-1, 2:] - lam_pad[:, 1:-1, :-2]
    )
    received = lax.all_to_all(marker_rows, "lat", split_axis=1, concat_axis=1, tiled=True)
    senders = lax.axis_size("lat")
    slot_total = received.shape[1]
    per_sender = slot_total // senders
    live = (jnp.arange(per_sender, dtype=jnp.int32)[None, :] < recv_counts[:, None]).reshape(-1)
    target = jnp.where(live, recv_cells, -1)
    block = math.gcd(slot_total, 512)
    blocks = slot_total // block
    cell_count = first_len * second_len
    rows_blocks = received.reshape(layers, blocks, block).transpose(1, 0, 2)
    target_blocks = target.reshape(blocks, block)
    cell_ids = jnp.arange(cell_count, dtype=jnp.int32)

    def deposit_block(total, item):
        rows_part, target_part = item
        onehot = (target_part[:, None] == cell_ids[None, :]).astype(jnp.bfloat16)
        return (total + jnp.dot(rows_part, onehot, preferred_element_type=jnp.float32), None)

    deposit, unused = lax.scan(
        deposit_block, jnp.zeros((layers, cell_count), jnp.float32), (rows_blocks, target_blocks)
    )
    deposit = deposit.reshape(layers, first_len, second_len)
    rhs = iterate + advect_coef * advect + deposit
    full_layers = radial_inverse.shape[0]
    columns = lax.all_to_all(rhs, "rad", split_axis=1, concat_axis=0, tiled=True)
    result = jnp.dot(
        radial_inverse, columns.reshape(full_layers, -1), precision=lax.Precision.HIGHEST
    )
    return result.reshape(columns.shape)


def solution(mesh):
    in_specs = (
        P("rad", "cap", "lat"),
        P(None, "rad", "cap", "lat"),
        P("rad", "cap", "lat"),
        P("rad", "cap", "lat"),
        P("rad", "cap", "lat"),
        P(),
        P("rad", ("cap", "lat")),
        P(("cap", "lat")),
        P(("cap", "lat")),
    )
    out_specs = P(None, ("cap", "rad"), "lat")
    return jax.shard_map(
        per_device, mesh=mesh, in_specs=in_specs, out_specs=out_specs, check_vma=False
    )
```

profile of v0, /device:TPU:1, one launch (start us, length us, event | category | flops | bytes accessed | tf_op | source)
XLA Modules:
  0.0 151.4 jit_solution(331933865882135294)
XLA Ops:
  2.1 4.0 %collective-permute-start = (f32[2,32,1,256]{3,2,1,0:T(1,128)S(1)}, f32[2,32,1,256]{3,2,1,0:T(1,128)S(1)}, u32[]{:S(2)}, u32[]{:S(2)}) collective-permute-start(f32[2,32,1,256]{3,2,1,0:T(1,128)S(1)} %get-tuple-element.62), channel_id=1, source_target_pairs={{0,8},{8,16},{16,24},{1,9},{9,17},{17,25},{2,10},{10,18},{18,26},{... | collective-permute-start | bytes 196616 | tf_op jit(solution)/shard_map/ppermute | solution.py:19
  7.4 3.7 %collective-permute-done.1 = f32[2,32,1,256]{3,2,1,0:T(1,128)S(1)} collective-permute-done((f32[2,32,1,256]{3,2,1,0:T(1,128)S(1)}, f32[2,32,1,256]{3,2,1,0:T(1,128)S(1)}, u32[]{:S(2)}, u32[]{:S(2)}) %collective-permute-start.1) | collective-permute-done | bytes 65568 | tf_op jit(solution)/shard_map/ppermute | solution.py:20
  15.3 5.1 %collective-permute-start.2 = (f32[2,32,34,1]{2,1,3,0:T(8,128)S(1)}, f32[2,32,34,1]{2,1,3,0:T(8,128)S(1)}, u32[]{:S(2)}, u32[]{:S(2)}) collective-permute-start(f32[2,32,34,1]{2,1,3,0:T(8,128)S(1)} %copy.28), channel_id=1, source_target_pairs={{0,2},{2,4},{4,6},{1,3},{3,5},{5,7},{8,10},{10,12},{12,14},{9,11},... | collective-permute-start | bytes 26120 | tf_op jit(solution)/shard_map/ppermute | solution.py:19
  29.2 4.3 %fusion.11 = f32[2,32,34,258]{3,2,1,0:T(8,128)S(1)} fusion(f32[1,32,32,256]{3,2,1,0:T(8,128)S(1)} %bitcast.53, f32[2,32,34,1]{3,2,1,0:T(8,128)} %copy.31, f32[2,32,1,256]{3,2,1,0:T(1,128)S(1)} %collective-permute-done.1, f32[1,32,32,256]{3,2,1,0:T(8,128)S(1)} %bitcast.60, f32[2,32,1,256]{3,2,1,0:T(1,128)S(1)} %collective-permute-done, f32[2,32,34,1]{3,2,1,0:T(8,128)} %copy.30), kind=kLoop, calls=%fused_computation.15 | loop fusion | flops 2807040 | bytes 4491264 | tf_op jit(solution)/shard_map/concatenate | solution.py:21
  34.7 2.0 %fusion.58 = f32[32,32,256]{2,1,0:T(8,128)S(1)} fusion(f32[32,32,256]{2,1,0:T(8,128)S(1)} %copy-done.2, f32[32,32,256]{2,1,0:T(8,128)S(1)} %convert_select_fusion, f32[32,34,258]{2,1,0:T(8,128)S(1)} %get-tuple-element.71, f32[32,34,258]{2,1,0:T(8,128)S(1)} %get-tuple-element.70), kind=kLoop, calls=%fused_computation.96 | loop fusion | flops 5505024 | bytes 11534336 | tf_op jit(solution)/shard_map/add | solution.py:58
  38.4 3.2 %collective-permute-start.4 = (f32[2,32,1,256]{3,2,1,0:T(1,128)}, f32[2,32,1,256]{3,2,1,0:T(1,128)S(1)}, u32[]{:S(2)}, u32[]{:S(2)}) collective-permute-start(f32[2,32,1,256]{3,2,1,0:T(1,128)} %get-tuple-element.80), channel_id=1, source_target_pairs={{0,8},{8,16},{16,24},{1,9},{9,17},{17,25},{2,10},{10,18},{18,26},{... | collective-permute-start | bytes 196616 | tf_op jit(solution)/shard_map/ppermute | solution.py:19
  43.5 3.3 %all-to-all-start = ((bf16[32,4,512]{2,0,1:T(8,128)(2,1)}), bf16[32,4,512]{2,0,1:T(8,128)(2,1)S(1)}, u32[]{:S(2)}, u32[]{:S(2)}) async-start(bf16[32,4,512]{2,0,1:T(8,128)(2,1)} %bitcast.46), calls=%async_computation | async-start | bytes 262144 | tf_op jit(solution)/shard_map/all_to_all | solution.py:62
  52.2 3.1 %collective-permute-start.6 = (f32[2,32,34,1]{2,1,3,0:T(8,128)S(1)}, f32[2,32,34,1]{2,1,3,0:T(8,128)S(1)}, u32[]{:S(2)}, u32[]{:S(2)}) collective-permute-start(f32[2,32,34,1]{2,1,3,0:T(8,128)S(1)} %copy.32), channel_id=1, source_target_pairs={{0,2},{2,4},{4,6},{1,3},{3,5},{5,7},{8,10},{10,12},{12,14},{9,11},... | collective-permute-start | bytes 26120 | tf_op jit(solution)/shard_map/ppermute | solution.py:19
  57.2 2.1 %collective-permute-start.7 = (f32[2,32,34,1]{2,1,3,0:T(8,128)S(1)}, f32[2,32,34,1]{2,1,3,0:T(8,128)}, u32[]{:S(2)}, u32[]{:S(2)}) collective-permute-start(f32[2,32,34,1]{2,1,3,0:T(8,128)S(1)} %copy.33), channel_id=1, source_target_pairs={{2,0},{4,2},{6,4},{3,1},{5,3},{7,5},{10,8},{12,10},{14,12},{11,9},... | collective-permute-start | bytes 26120 | tf_op jit(solution)/shard_map/ppermute | solution.py:20
  62.5 2.4 %copy.35 = f32[2,32,34,1]{3,2,1,0:T(8,128)} copy(f32[2,32,34,1]{2,1,3,0:T(8,128)} %collective-permute-done.7) | data formatting | bytes 17408 | tf_op jit(solution)/shard_map/ppermute | solution.py:20
  64.9 4.4 %fusion.15 = f32[2,32,34,258]{3,2,1,0:T(8,128)S(1)} fusion(f32[1,32,32,256]{3,2,1,0:T(8,128)S(1)} %bitcast.55, f32[2,32,34,1]{3,2,1,0:T(8,128)} %copy.35, f32[2,32,1,256]{3,2,1,0:T(1,128)S(1)} %collective-permute-done.5, f32[1,32,32,256]{3,2,1,0:T(8,128)} %bitcast.66, f32[2,32,1,256]{3,2,1,0:T(1,128)S(1)} %collective-permute-done.4, f32[2,32,34,1]{3,2,1,0:T(8,128)} %copy.34), kind=kLoop, calls=%fused_computation.19 | loop fusion | flops 2807040 | bytes 4491264 | tf_op jit(solution)/shard_map/concatenate | solution.py:21
  73.9 3.4 %collective-permute-start.8 = (f32[2,32,1,256]{3,2,1,0:T(1,128)S(1)}, f32[2,32,1,256]{3,2,1,0:T(1,128)S(1)}, u32[]{:S(2)}, u32[]{:S(2)}) collective-permute-start(f32[2,32,1,256]{3,2,1,0:T(1,128)S(1)} %get-tuple-element.78), channel_id=1, source_target_pairs={{0,8},{8,16},{16,24},{1,9},{9,17},{17,25},{2,10},{10,18},{18,26},{... | collective-permute-start | bytes 196616 | tf_op jit(solution)/shard_map/ppermute | solution.py:19
  78.7 3.7 %collective-permute-done.9 = f32[2,32,1,256]{3,2,1,0:T(1,128)S(1)} collective-permute-done((f32[2,32,1,256]{3,2,1,0:T(1,128)S(1)}, f32[2,32,1,256]{3,2,1,0:T(1,128)S(1)}, u32[]{:S(2)}, u32[]{:S(2)}) %collective-permute-start.9) | collective-permute-done | bytes 65568 | tf_op jit(solution)/shard_map/ppermute | solution.py:20
  87.7 3.6 %collective-permute-start.10 = (f32[2,32,34,1]{2,1,3,0:T(8,128)S(1)}, f32[2,32,34,1]{2,1,3,0:T(8,128)S(1)}, u32[]{:S(2)}, u32[]{:S(2)}) collective-permute-start(f32[2,32,34,1]{2,1,3,0:T(8,128)S(1)} %copy.36), channel_id=1, source_target_pairs={{0,2},{2,4},{4,6},{1,3},{3,5},{5,7},{8,10},{10,12},{12,14},{9,11},... | collective-permute-start | bytes 26120 | tf_op jit(solution)/shard_map/ppermute | solution.py:19
  93.1 2.1 %collective-permute-start.11 = (f32[2,32,34,1]{2,1,3,0:T(8,128)S(1)}, f32[2,32,34,1]{2,1,3,0:T(8,128)S(1)}, u32[]{:S(2)}, u32[]{:S(2)}) collective-permute-start(f32[2,32,34,1]{2,1,3,0:T(8,128)S(1)} %copy.37), channel_id=1, source_target_pairs={{2,0},{4,2},{6,4},{3,1},{5,3},{7,5},{10,8},{12,10},{14,12},{11,9},... | collective-permute-start | bytes 26120 | tf_op jit(solution)/shard_map/ppermute | solution.py:20
  95.3 21.3 %while.11 = (s32[]{:T(128)}, f32[32,8192]{1,0:T(8,128)}, bf16[4,32,512]{2,1,0:T(8,128)(2,1)S(1)}, s32[4,512]{1,0:T(4,128)S(1)}, s32[]{:T(128)}, /*index=5*/s32[]{:T(128)}) while((s32[]{:T(128)}, f32[32,8192]{1,0:T(8,128)}, bf16[4,32,512]{2,1,0:T(8,128)(2,1)S(1)}, s32[4,512]{1,0:T(4,128)S(1)}, s32[]{:T(128)}, ...), condition=%wide.region_1.2_spmd.clone, body=%wide.region_0.1_spmd.clone.sunk | while | flops 273154048 | bytes 2136151 | solution.py:80
  95.3 4.4 %fusion.82 = f32[32,8192]{1,0:T(8,128)} fusion(s32[512]{0:T(512)S(1)} %bitcast.74, f32[32,8192]{1,0:T(8,128)} %get-tuple-element.116, pred[]{:T(512)S(6)} %compare.3, bf16[4,32,512]{2,1,0:T(8,128)(2,1)S(1)} %get-tuple-element.123, s32[]{:T(128)} %get-tuple-element.115), kind=kOutput, calls=%fused_computation.3.clone.1 | convolution fusion | flops 273154048 | bytes 2131973 | tf_op jit(solution)/shard_map/while/body/eval_jaxpr/dot_general | solution.py:78
  99.7 5.6 %fusion.82 = f32[32,8192]{1,0:T(8,128)} fusion(s32[512]{0:T(512)S(1)} %bitcast.74, f32[32,8192]{1,0:T(8,128)} %get-tuple-element.116, pred[]{:T(512)S(6)} %compare.3, bf16[4,32,512]{2,1,0:T(8,128)(2,1)S(1)} %get-tuple-element.123, s32[]{:T(128)} %get-tuple-element.115), kind=kOutput, calls=%fused_computation.3.clone.1 | convolution fusion | flops 273154048 | bytes 2131973 | tf_op jit(solution)/shard_map/while/body/eval_jaxpr/dot_general | solution.py:78
  105.4 5.6 %fusion.82 = f32[32,8192]{1,0:T(8,128)} fusion(s32[512]{0:T(512)S(1)} %bitcast.74, f32[32,8192]{1,0:T(8,128)} %get-tuple-element.116, pred[]{:T(512)S(6)} %compare.3, bf16[4,32,512]{2,1,0:T(8,128)(2,1)S(1)} %get-tuple-element.123, s32[]{:T(128)} %get-tuple-element.115), kind=kOutput, calls=%fused_computation.3.clone.1 | convolution fusion | flops 273154048 | bytes 2131973 | tf_op jit(solution)/shard_map/while/body/eval_jaxpr/dot_general | solution.py:78
  111.0 5.6 %fusion.82 = f32[32,8192]{1,0:T(8,128)} fusion(s32[512]{0:T(512)S(1)} %bitcast.74, f32[32,8192]{1,0:T(8,128)} %get-tuple-element.116, pred[]{:T(512)S(6)} %compare.3, bf16[4,32,512]{2,1,0:T(8,128)(2,1)S(1)} %get-tuple-element.123, s32[]{:T(128)} %get-tuple-element.115), kind=kOutput, calls=%fused_computation.3.clone.1 | convolution fusion | flops 273154048 | bytes 2131973 | tf_op jit(solution)/shard_map/while/body/eval_jaxpr/dot_general | solution.py:78
  116.6 2.5 %copy.45 = f32[4,8,32,256]{3,2,1,0:T(8,128)} copy(f32[4,8,32,256]{3,1,2,0:T(8,128)} %bitcast.71) | data formatting | bytes 2097152
  122.4 4.4 %fusion.19 = f32[2,32,34,258]{3,2,1,0:T(8,128)S(1)} fusion(f32[1,32,32,256]{3,2,1,0:T(8,128)S(1)} %bitcast.57, f32[2,32,34,1]{3,2,1,0:T(8,128)} %copy.39, f32[2,32,1,256]{3,2,1,0:T(1,128)S(1)} %collective-permute-done.9, f32[1,32,32,256]{3,2,1,0:T(8,128)} %bitcast.63, f32[2,32,1,256]{3,2,1,0:T(1,128)S(1)} %collective-permute-done.8, f32[2,32,34,1]{3,2,1,0:T(8,128)} %copy.38), kind=kLoop, calls=%fused_computation.23 | loop fusion | flops 2807040 | bytes 4491264 | tf_op jit(solution)/shard_map/concatenate | solution.py:21
  129.0 3.0 %bitcast_add_fusion = f32[32,32,256]{2,1,0:T(8,128)S(1)} fusion(f32[4,8,32,256]{3,2,1,0:T(8,128)S(1)} %copy-done.9, f32[32,32,256]{2,1,0:T(8,128)S(1)} %copy-done.4, f32[32,32,256]{2,1,0:T(8,128)S(1)} %copy-done.6, f32[32,34,258]{2,1,0:T(8,128)S(1)} %get-tuple-element.67, f32[32,32,256]{2,1,0:T(8,128)S(1)} %convert_select_fusion, ...), kind=kLoop, calls=%fused_computation.47 | loop fusion | flops 8126464 | bytes 18874368 | tf_op jit(solution)/shard_map/add | solution.py:84
  132.6 15.1 %all_to_all.24 = f32[32,32,256]{2,0,1:T(8,128)S(1)} all-to-all(f32[32,32,256]{2,0,1:T(8,128)S(1)} %copy.41), channel_id=1, replica_groups=mesh['cap'=4,'lat'=4,'rad'=2] {'rad'}, dimensions={1} | all-to-all | bytes 2097152 | tf_op jit(solution)/shard_map/all_to_all | solution.py:86
  (83 shorter events, 54.2 us)
Async XLA Ops:
  0.0 149.0 %copy-start = (f32[64,64]{1,0:T(8,128)S(1)}, f32[64,64]{1,0:T(8,128)}, u32[]{:S(2)}) copy-start(f32[64,64]{1,0:T(8,128)} %param.16) | copy-start | bytes 49156
  0.0 1.9 %copy-start.1 = (f32[32,32,256]{2,1,0:T(8,128)S(1)}, f32[32,32,256]{2,1,0:T(8,128)}, u32[]{:S(2)}) copy-start(f32[32,32,256]{2,1,0:T(8,128)} %param.11) | copy-start | bytes 3145732
  2.1 5.4 %collective-permute-start = (f32[2,32,1,256]{3,2,1,0:T(1,128)S(1)}, f32[2,32,1,256]{3,2,1,0:T(1,128)S(1)}, u32[]{:S(2)}, u32[]{:S(2)}) collective-permute-start(f32[2,32,1,256]{3,2,1,0:T(1,128)S(1)} %get-tuple-element.62), channel_id=1, source_target_pairs={{0,8},{8,16},{16,24},{1,9},{9,17},{17,25},{2,10},{10,18},{18,26},{... | collective-permute-start | bytes 196616 | tf_op jit(solution)/shard_map/ppermute | solution.py:19
  6.1 5.0 %collective-permute-start.1 = (f32[2,32,1,256]{3,2,1,0:T(1,128)S(1)}, f32[2,32,1,256]{3,2,1,0:T(1,128)S(1)}, u32[]{:S(2)}, u32[]{:S(2)}) collective-permute-start(f32[2,32,1,256]{3,2,1,0:T(1,128)S(1)} %get-tuple-element.82), channel_id=1, source_target_pairs={{8,0},{16,8},{24,16},{9,1},{17,9},{25,17},{10,2},{18,10},{26,18},{... | collective-permute-start | bytes 196616 | tf_op jit(solution)/shard_map/ppermute | solution.py:20
  15.3 8.9 %collective-permute-start.2 = (f32[2,32,34,1]{2,1,3,0:T(8,128)S(1)}, f32[2,32,34,1]{2,1,3,0:T(8,128)S(1)}, u32[]{:S(2)}, u32[]{:S(2)}) collective-permute-start(f32[2,32,34,1]{2,1,3,0:T(8,128)S(1)} %copy.28), channel_id=1, source_target_pairs={{0,2},{2,4},{4,6},{1,3},{3,5},{5,7},{8,10},{10,12},{12,14},{9,11},... | collective-permute-start | bytes 26120 | tf_op jit(solution)/shard_map/ppermute | solution.py:19
  22.3 5.2 %collective-permute-start.3 = (f32[2,32,34,1]{2,1,3,0:T(8,128)S(1)}, f32[2,32,34,1]{2,1,3,0:T(8,128)S(1)}, u32[]{:S(2)}, u32[]{:S(2)}) collective-permute-start(f32[2,32,34,1]{2,1,3,0:T(8,128)S(1)} %copy.29), channel_id=1, source_target_pairs={{2,0},{4,2},{6,4},{3,1},{5,3},{7,5},{10,8},{12,10},{14,12},{11,9},... | collective-permute-start | bytes 26120 | tf_op jit(solution)/shard_map/ppermute | solution.py:20
  33.4 1.2 copy-start.2
  34.7 8.2 %copy-start.11 = (bf16[32,2048]{1,0:T(8,128)(2,1)S(1)}, bf16[32,2048]{1,0:T(8,128)(2,1)}, u32[]{:S(2)}) copy-start(bf16[32,2048]{1,0:T(8,128)(2,1)} %param.17) | copy-start | bytes 393220
  38.4 8.5 %collective-permute-start.4 = (f32[2,32,1,256]{3,2,1,0:T(1,128)}, f32[2,32,1,256]{3,2,1,0:T(1,128)S(1)}, u32[]{:S(2)}, u32[]{:S(2)}) collective-permute-start(f32[2,32,1,256]{3,2,1,0:T(1,128)} %get-tuple-element.80), channel_id=1, source_target_pairs={{0,8},{8,16},{16,24},{1,9},{9,17},{17,25},{2,10},{10,18},{18,26},{... | collective-permute-start | bytes 196616 | tf_op jit(solution)/shard_map/ppermute | solution.py:19
  41.6 5.3 %collective-permute-start.5 = (f32[2,32,1,256]{3,2,1,0:T(1,128)S(1)}, f32[2,32,1,256]{3,2,1,0:T(1,128)S(1)}, u32[]{:S(2)}, u32[]{:S(2)}) collective-permute-start(f32[2,32,1,256]{3,2,1,0:T(1,128)S(1)} %get-tuple-element.81), channel_id=1, source_target_pairs={{8,0},{16,8},{24,16},{9,1},{17,9},{25,17},{10,2},{18,10},{26,18},{... | collective-permute-start | bytes 196616 | tf_op jit(solution)/shard_map/ppermute | solution.py:20
  43.5 51.7 %all-to-all-start = ((bf16[32,4,512]{2,0,1:T(8,128)(2,1)}), bf16[32,4,512]{2,0,1:T(8,128)(2,1)S(1)}, u32[]{:S(2)}, u32[]{:S(2)}) async-start(bf16[32,4,512]{2,0,1:T(8,128)(2,1)} %bitcast.46), calls=%async_computation | async-start | bytes 262144 | tf_op jit(solution)/shard_map/all_to_all | solution.py:62
  50.4 9.0 %copy-start.13 = (s32[4]{0:T(128)S(1)}, s32[4]{0:T(128)}, u32[]{:S(2)}) copy-start(s32[4]{0:T(128)} %param.19) | copy-start | bytes 52
  52.2 7.2 %collective-permute-start.6 = (f32[2,32,34,1]{2,1,3,0:T(8,128)S(1)}, f32[2,32,34,1]{2,1,3,0:T(8,128)S(1)}, u32[]{:S(2)}, u32[]{:S(2)}) collective-permute-start(f32[2,32,34,1]{2,1,3,0:T(8,128)S(1)} %copy.32), channel_id=1, source_target_pairs={{0,2},{2,4},{4,6},{1,3},{3,5},{5,7},{8,10},{10,12},{12,14},{9,11},... | collective-permute-start | bytes 26120 | tf_op jit(solution)/shard_map/ppermute | solution.py:19
  57.2 5.3 %collective-permute-start.7 = (f32[2,32,34,1]{2,1,3,0:T(8,128)S(1)}, f32[2,32,34,1]{2,1,3,0:T(8,128)}, u32[]{:S(2)}, u32[]{:S(2)}) collective-permute-start(f32[2,32,34,1]{2,1,3,0:T(8,128)S(1)} %copy.33), channel_id=1, source_target_pairs={{2,0},{4,2},{6,4},{3,1},{5,3},{7,5},{10,8},{12,10},{14,12},{11,9},... | collective-permute-start | bytes 26120 | tf_op jit(solution)/shard_map/ppermute | solution.py:20
  69.4 1.5 %copy-start.8 = (f32[32,32,256]{2,1,0:T(8,128)S(1)}, f32[32,32,256]{2,1,0:T(8,128)}, u32[]{:S(2)}) copy-start(f32[32,32,256]{2,1,0:T(8,128)} %copy-done.7) | copy-start | bytes 3145732
  70.9 7.7 %copy-start.12 = (s32[2048]{0:T(1024)S(1)}, s32[2048]{0:T(1024)}, u32[]{:S(2)}) copy-start(s32[2048]{0:T(1024)} %param.18) | copy-start | bytes 24580
  73.9 4.8 %collective-permute-start.8 = (f32[2,32,1,256]{3,2,1,0:T(1,128)S(1)}, f32[2,32,1,256]{3,2,1,0:T(1,128)S(1)}, u32[]{:S(2)}, u32[]{:S(2)}) collective-permute-start(f32[2,32,1,256]{3,2,1,0:T(1,128)S(1)} %get-tuple-element.78), channel_id=1, source_target_pairs={{0,8},{8,16},{16,24},{1,9},{9,17},{17,25},{2,10},{10,18},{18,26},{... | collective-permute-start | bytes 196616 | tf_op jit(solution)/shard_map/ppermute | solution.py:19
  77.3 5.0 %collective-permute-start.9 = (f32[2,32,1,256]{3,2,1,0:T(1,128)S(1)}, f32[2,32,1,256]{3,2,1,0:T(1,128)S(1)}, u32[]{:S(2)}, u32[]{:S(2)}) collective-permute-start(f32[2,32,1,256]{3,2,1,0:T(1,128)S(1)} %get-tuple-element.79), channel_id=1, source_target_pairs={{8,0},{16,8},{24,16},{9,1},{17,9},{25,17},{10,2},{18,10},{26,18},{... | collective-permute-start | bytes 196616 | tf_op jit(solution)/shard_map/ppermute | solution.py:20
  87.7 31.5 %collective-permute-start.10 = (f32[2,32,34,1]{2,1,3,0:T(8,128)S(1)}, f32[2,32,34,1]{2,1,3,0:T(8,128)S(1)}, u32[]{:S(2)}, u32[]{:S(2)}) collective-permute-start(f32[2,32,34,1]{2,1,3,0:T(8,128)S(1)} %copy.36), channel_id=1, source_target_pairs={{0,2},{2,4},{4,6},{1,3},{3,5},{5,7},{8,10},{10,12},{12,14},{9,11},... | collective-permute-start | bytes 26120 | tf_op jit(solution)/shard_map/ppermute | solution.py:19
  93.1 27.7 %collective-permute-start.11 = (f32[2,32,34,1]{2,1,3,0:T(8,128)S(1)}, f32[2,32,34,1]{2,1,3,0:T(8,128)S(1)}, u32[]{:S(2)}, u32[]{:S(2)}) collective-permute-start(f32[2,32,34,1]{2,1,3,0:T(8,128)S(1)} %copy.37), channel_id=1, source_target_pairs={{2,0},{4,2},{6,4},{3,1},{5,3},{7,5},{10,8},{12,10},{14,12},{11,9},... | collective-permute-start | bytes 26120 | tf_op jit(solution)/shard_map/ppermute | solution.py:20
  126.8 1.2 copy-start.4
  126.9 1.5 %copy-start.6 = (f32[32,32,256]{2,1,0:T(8,128)S(1)}, f32[32,32,256]{2,1,0:T(8,128)}, u32[]{:S(2)}) copy-start(f32[32,32,256]{2,1,0:T(8,128)} %copy-done.5) | copy-start | bytes 3145732
  126.9 1.8 %copy-start.9 = (f32[4,8,32,256]{3,2,1,0:T(8,128)S(1)}, f32[4,8,32,256]{3,2,1,0:T(8,128)}, u32[]{:S(2)}) copy-start(f32[4,8,32,256]{3,2,1,0:T(8,128)} %copy.45) | copy-start | bytes 3145732
  126.9 2.1 %copy-start.10 = (bf16[2,32,32,256]{3,2,1,0:T(8,128)(2,1)S(1)}, bf16[2,32,32,256]{3,2,1,0:T(8,128)(2,1)}, u32[]{:S(2)}) copy-start(bf16[2,32,32,256]{3,2,1,0:T(8,128)(2,1)} %param.12) | copy-start | bytes 3145732
  (3 other events, 3.2 us)
where the time goes:
time: 153 us; the launch traced here: 151 us
  local copies, waits for them, and re-layouts  40.6 us (27%)
  starting transfers between devices  35.8 us (23%)
  other arithmetic  26.6 us (17%)
  matrix products  22.4 us (15%)
  blocking collectives  15.1 us (10%)
  waiting for transfers between devices  10.5 us (7%)
    ppermute x6, starting transfers between devices, extended(): before = lax.ppermute(last, axis, up)  22.4 us
    dot_general x4, matrix products, deposit_block(): jnp.dot(rows_part, onehot, preferred_element_type=jnp.float32)  21.3 us
    concatenate x6, other arithmetic, extended(): x = jnp.concatenate([before, x, after], axis=dim)  16.7 us
    all_to_all x1, blocking collectives, per_device(): lax.all_to_all(rhs, 'rad', split_axis=1, concat_axis=0, tiled=True)  15.1 us
    slice x6, local copies, waits for them, and re-layouts, extended(): last = lax.slice_in_dim(x, length - width, length, axis=dim)  11.2 us
    ppermute x6, waiting for transfers between devices, extended(): after = lax.ppermute(first, axis, down)  10.5 us
    unnamed x32, local copies, waits for them, and re-layouts  10.5 us
    ppermute x6, starting transfers between devices, extended(): after = lax.ppermute(first, axis, down)  10 us
  transfers between devices with their start and end apart: 13, of which 4 were waited for; matrix products, arithmetic and copies ran while one was open for 36% of the time, Pallas kernels for 0%

commit v1 on v0

--- a/solution.py
+++ b/solution.py
@@ -1,3 +1,4 @@
+import functools
 import math
 import jax
 import jax.numpy as jnp
@@ -7,6 +8,17 @@
 PICARD = 3
 relax_coef = 0.25
 advect_coef = 0.1
+
+
+def ranges_replace(x_local, link_axis):
+    response = lax.axis_size(link_axis)
+    found_now = jnp.split(x_local, response, axis=1)
+    met_up = jnp.stack(found_now)
+    local_next = lax.all_to_all(met_up, axis_name=link_axis, split_axis=0, concat_axis=0)
+    return jnp.concatenate(local_next, axis=0)
+
+
+settle_ticks_over_axis = functools.partial(ranges_replace, link_axis="rad")
 
 
 def extended(x, sides, width):
@@ -83,7 +95,7 @@
     deposit = deposit.reshape(layers, first_len, second_len)
     rhs = iterate + advect_coef * advect + deposit
     full_layers = radial_inverse.shape[0]
-    columns = lax.all_to_all(rhs, "rad", split_axis=1, concat_axis=0, tiled=True)
+    columns = settle_ticks_over_axis(rhs)
     result = jnp.dot(
         radial_inverse, columns.reshape(full_layers, -1), precision=lax.Precision.HIGHEST
     )

time: 153 us -> 151 us (0.987)
  no operation moved by 1% of the time
where the time goes in v1:
time: 151 us; the launch traced here: 150 us
  local copies, waits for them, and re-layouts  39.4 us (26%)
  starting transfers between devices  35.8 us (24%)
  other arithmetic  26.6 us (18%)
  matrix products  22.4 us (15%)
  blocking collectives  15.1 us (10%)
  waiting for transfers between devices  10.5 us (7%)
    ppermute x6, starting transfers between devices, extended(): before = lax.ppermute(last, axis, up)  22.5 us
    dot_general x4, matrix products, deposit_block(): jnp.dot(rows_part, onehot, preferred_element_type=jnp.float32)  21.3 us
    concatenate x6, other arithmetic, extended(): x = jnp.concatenate([before, x, after], axis=dim)  16.7 us
    all_to_all x1, blocking collectives, ranges_replace(): lax.all_to_all(met_up, axis_name=link_axis, split_axis=0, concat_axis=0)  15.1 us
    slice x6, local copies, waits for them, and re-layouts, extended(): last = lax.slice_in_dim(x, length - width, length, axis=dim)  11.2 us
    unnamed x32, local copies, waits for them, and re-layouts  10.5 us
    ppermute x6, waiting for transfers between devices, extended(): after = lax.ppermute(first, axis, down)  10.5 us
    ppermute x6, starting transfers between devices, extended(): after = lax.ppermute(first, axis, down)  10 us
  transfers between devices with their start and end apart: 13, of which 4 were waited for; matrix products, arithmetic and copies ran while one was open for 36% of the time, Pallas kernels for 0%

profile of v1, /device:TPU:1, one launch (start us, length us, event | category | flops | bytes accessed | tf_op | source)
XLA Modules:
  0.0 150.3 jit_solution(2071247404623888754)
XLA Ops:
  2.1 4.0 %collective-permute-start = (f32[2,32,1,256]{3,2,1,0:T(1,128)S(1)}, f32[2,32,1,256]{3,2,1,0:T(1,128)S(1)}, u32[]{:S(2)}, u32[]{:S(2)}) collective-permute-start(f32[2,32,1,256]{3,2,1,0:T(1,128)S(1)} %get-tuple-element.62), channel_id=1, source_target_pairs={{0,8},{8,16},{16,24},{1,9},{9,17},{17,25},{2,10},{10,18},{18,26},{... | collective-permute-start | bytes 196616 | tf_op jit(solution)/shard_map/ppermute | solution.py:31
  7.4 3.7 %collective-permute-done.1 = f32[2,32,1,256]{3,2,1,0:T(1,128)S(1)} collective-permute-done((f32[2,32,1,256]{3,2,1,0:T(1,128)S(1)}, f32[2,32,1,256]{3,2,1,0:T(1,128)S(1)}, u32[]{:S(2)}, u32[]{:S(2)}) %collective-permute-start.1) | collective-permute-done | bytes 65568 | tf_op jit(solution)/shard_map/ppermute | solution.py:32
  15.3 5.1 %collective-permute-start.2 = (f32[2,32,34,1]{2,1,3,0:T(8,128)S(1)}, f32[2,32,34,1]{2,1,3,0:T(8,128)S(1)}, u32[]{:S(2)}, u32[]{:S(2)}) collective-permute-start(f32[2,32,34,1]{2,1,3,0:T(8,128)S(1)} %copy.25), channel_id=1, source_target_pairs={{0,2},{2,4},{4,6},{1,3},{3,5},{5,7},{8,10},{10,12},{12,14},{9,11},... | collective-permute-start | bytes 26120 | tf_op jit(solution)/shard_map/ppermute | solution.py:31
  29.2 4.3 %fusion.11 = f32[2,32,34,258]{3,2,1,0:T(8,128)S(1)} fusion(f32[1,32,32,256]{3,2,1,0:T(8,128)S(1)} %bitcast.55, f32[2,32,34,1]{3,2,1,0:T(8,128)} %copy.28, f32[2,32,1,256]{3,2,1,0:T(1,128)S(1)} %collective-permute-done.1, f32[1,32,32,256]{3,2,1,0:T(8,128)S(1)} %bitcast.62, f32[2,32,1,256]{3,2,1,0:T(1,128)S(1)} %collective-permute-done, f32[2,32,34,1]{3,2,1,0:T(8,128)} %copy.27), kind=kLoop, calls=%fused_computation.15 | loop fusion | flops 2807040 | bytes 4491264 | tf_op jit(solution)/shard_map/concatenate | solution.py:33
  34.7 2.0 %fusion.58 = f32[32,32,256]{2,1,0:T(8,128)S(1)} fusion(f32[32,32,256]{2,1,0:T(8,128)S(1)} %copy-done.2, f32[32,32,256]{2,1,0:T(8,128)S(1)} %convert_select_fusion, f32[32,34,258]{2,1,0:T(8,128)S(1)} %get-tuple-element.71, f32[32,34,258]{2,1,0:T(8,128)S(1)} %get-tuple-element.70), kind=kLoop, calls=%fused_computation.96 | loop fusion | flops 5505024 | bytes 11534336 | tf_op jit(solution)/shard_map/add | solution.py:70
  38.4 3.2 %collective-permute-start.4 = (f32[2,32,1,256]{3,2,1,0:T(1,128)}, f32[2,32,1,256]{3,2,1,0:T(1,128)S(1)}, u32[]{:S(2)}, u32[]{:S(2)}) collective-permute-start(f32[2,32,1,256]{3,2,1,0:T(1,128)} %get-tuple-element.82), channel_id=1, source_target_pairs={{0,8},{8,16},{16,24},{1,9},{9,17},{17,25},{2,10},{10,18},{18,26},{... | collective-permute-start | bytes 196616 | tf_op jit(solution)/shard_map/ppermute | solution.py:31
  43.5 3.3 %all-to-all-start = ((bf16[32,4,512]{2,0,1:T(8,128)(2,1)}), bf16[32,4,512]{2,0,1:T(8,128)(2,1)S(1)}, u32[]{:S(2)}, u32[]{:S(2)}) async-start(bf16[32,4,512]{2,0,1:T(8,128)(2,1)} %bitcast.48), calls=%async_computation | async-start | bytes 262144 | tf_op jit(solution)/shard_map/all_to_all | solution.py:74
  52.2 3.1 %collective-permute-start.6 = (f32[2,32,34,1]{2,1,3,0:T(8,128)S(1)}, f32[2,32,34,1]{2,1,3,0:T(8,128)S(1)}, u32[]{:S(2)}, u32[]{:S(2)}) collective-permute-start(f32[2,32,34,1]{2,1,3,0:T(8,128)S(1)} %copy.29), channel_id=1, source_target_pairs={{0,2},{2,4},{4,6},{1,3},{3,5},{5,7},{8,10},{10,12},{12,14},{9,11},... | collective-permute-start | bytes 26120 | tf_op jit(solution)/shard_map/ppermute | solution.py:31
  57.2 2.1 %collective-permute-start.7 = (f32[2,32,34,1]{2,1,3,0:T(8,128)S(1)}, f32[2,32,34,1]{2,1,3,0:T(8,128)}, u32[]{:S(2)}, u32[]{:S(2)}) collective-permute-start(f32[2,32,34,1]{2,1,3,0:T(8,128)S(1)} %copy.30), channel_id=1, source_target_pairs={{2,0},{4,2},{6,4},{3,1},{5,3},{7,5},{10,8},{12,10},{14,12},{11,9},... | collective-permute-start | bytes 26120 | tf_op jit(solution)/shard_map/ppermute | solution.py:32
  62.6 2.4 %copy.32 = f32[2,32,34,1]{3,2,1,0:T(8,128)} copy(f32[2,32,34,1]{2,1,3,0:T(8,128)} %collective-permute-done.7) | data formatting | bytes 17408 | tf_op jit(solution)/shard_map/ppermute | solution.py:32
  64.9 4.4 %fusion.15 = f32[2,32,34,258]{3,2,1,0:T(8,128)S(1)} fusion(f32[1,32,32,256]{3,2,1,0:T(8,128)S(1)} %bitcast.57, f32[2,32,34,1]{3,2,1,0:T(8,128)} %copy.32, f32[2,32,1,256]{3,2,1,0:T(1,128)S(1)} %collective-permute-done.5, f32[1,32,32,256]{3,2,1,0:T(8,128)} %bitcast.68, f32[2,32,1,256]{3,2,1,0:T(1,128)S(1)} %collective-permute-done.4, f32[2,32,34,1]{3,2,1,0:T(8,128)} %copy.31), kind=kLoop, calls=%fused_computation.19 | loop fusion | flops 2807040 | bytes 4491264 | tf_op jit(solution)/shard_map/concatenate | solution.py:33
  73.9 3.4 %collective-permute-start.8 = (f32[2,32,1,256]{3,2,1,0:T(1,128)S(1)}, f32[2,32,1,256]{3,2,1,0:T(1,128)S(1)}, u32[]{:S(2)}, u32[]{:S(2)}) collective-permute-start(f32[2,32,1,256]{3,2,1,0:T(1,128)S(1)} %get-tuple-element.80), channel_id=1, source_target_pairs={{0,8},{8,16},{16,24},{1,9},{9,17},{17,25},{2,10},{10,18},{18,26},{... | collective-permute-start | bytes 196616 | tf_op jit(solution)/shard_map/ppermute | solution.py:31
  78.7 3.7 %collective-permute-done.9 = f32[2,32,1,256]{3,2,1,0:T(1,128)S(1)} collective-permute-done((f32[2,32,1,256]{3,2,1,0:T(1,128)S(1)}, f32[2,32,1,256]{3,2,1,0:T(1,128)S(1)}, u32[]{:S(2)}, u32[]{:S(2)}) %collective-permute-start.9) | collective-permute-done | bytes 65568 | tf_op jit(solution)/shard_map/ppermute | solution.py:32
  87.7 3.6 %collective-permute-start.10 = (f32[2,32,34,1]{2,1,3,0:T(8,128)S(1)}, f32[2,32,34,1]{2,1,3,0:T(8,128)S(1)}, u32[]{:S(2)}, u32[]{:S(2)}) collective-permute-start(f32[2,32,34,1]{2,1,3,0:T(8,128)S(1)} %copy.33), channel_id=1, source_target_pairs={{0,2},{2,4},{4,6},{1,3},{3,5},{5,7},{8,10},{10,12},{12,14},{9,11},... | collective-permute-start | bytes 26120 | tf_op jit(solution)/shard_map/ppermute | solution.py:31
  93.1 2.1 %collective-permute-start.11 = (f32[2,32,34,1]{2,1,3,0:T(8,128)S(1)}, f32[2,32,34,1]{2,1,3,0:T(8,128)S(1)}, u32[]{:S(2)}, u32[]{:S(2)}) collective-permute-start(f32[2,32,34,1]{2,1,3,0:T(8,128)S(1)} %copy.34), channel_id=1, source_target_pairs={{2,0},{4,2},{6,4},{3,1},{5,3},{7,5},{10,8},{12,10},{14,12},{11,9},... | collective-permute-start | bytes 26120 | tf_op jit(solution)/shard_map/ppermute | solution.py:32
  95.3 21.3 %while.11 = (s32[]{:T(128)}, f32[32,8192]{1,0:T(8,128)}, bf16[4,32,512]{2,1,0:T(8,128)(2,1)S(1)}, s32[4,512]{1,0:T(4,128)S(1)}, s32[]{:T(128)}, /*index=5*/s32[]{:T(128)}) while((s32[]{:T(128)}, f32[32,8192]{1,0:T(8,128)}, bf16[4,32,512]{2,1,0:T(8,128)(2,1)S(1)}, s32[4,512]{1,0:T(4,128)S(1)}, s32[]{:T(128)}, ...), condition=%wide.region_1.2_spmd.clone, body=%wide.region_0.1_spmd.clone.sunk | while | flops 273154048 | bytes 2136151 | solution.py:92
  95.3 4.4 %fusion.82 = f32[32,8192]{1,0:T(8,128)} fusion(s32[512]{0:T(512)S(1)} %bitcast.75, f32[32,8192]{1,0:T(8,128)} %get-tuple-element.118, pred[]{:T(512)S(6)} %compare.3, bf16[4,32,512]{2,1,0:T(8,128)(2,1)S(1)} %get-tuple-element.125, s32[]{:T(128)} %get-tuple-element.117), kind=kOutput, calls=%fused_computation.3.clone.1 | convolution fusion | flops 273154048 | bytes 2131973 | tf_op jit(solution)/shard_map/while/body/eval_jaxpr/dot_general | solution.py:90
  99.8 5.6 %fusion.82 = f32[32,8192]{1,0:T(8,128)} fusion(s32[512]{0:T(512)S(1)} %bitcast.75, f32[32,8192]{1,0:T(8,128)} %get-tuple-element.118, pred[]{:T(512)S(6)} %compare.3, bf16[4,32,512]{2,1,0:T(8,128)(2,1)S(1)} %get-tuple-element.125, s32[]{:T(128)} %get-tuple-element.117), kind=kOutput, calls=%fused_computation.3.clone.1 | convolution fusion | flops 273154048 | bytes 2131973 | tf_op jit(solution)/shard_map/while/body/eval_jaxpr/dot_general | solution.py:90
  105.4 5.6 %fusion.82 = f32[32,8192]{1,0:T(8,128)} fusion(s32[512]{0:T(512)S(1)} %bitcast.75, f32[32,8192]{1,0:T(8,128)} %get-tuple-element.118, pred[]{:T(512)S(6)} %compare.3, bf16[4,32,512]{2,1,0:T(8,128)(2,1)S(1)} %get-tuple-element.125, s32[]{:T(128)} %get-tuple-element.117), kind=kOutput, calls=%fused_computation.3.clone.1 | convolution fusion | flops 273154048 | bytes 2131973 | tf_op jit(solution)/shard_map/while/body/eval_jaxpr/dot_general | solution.py:90
  111.0 5.6 %fusion.82 = f32[32,8192]{1,0:T(8,128)} fusion(s32[512]{0:T(512)S(1)} %bitcast.75, f32[32,8192]{1,0:T(8,128)} %get-tuple-element.118, pred[]{:T(512)S(6)} %compare.3, bf16[4,32,512]{2,1,0:T(8,128)(2,1)S(1)} %get-tuple-element.125, s32[]{:T(128)} %get-tuple-element.117), kind=kOutput, calls=%fused_computation.3.clone.1 | convolution fusion | flops 273154048 | bytes 2131973 | tf_op jit(solution)/shard_map/while/body/eval_jaxpr/dot_general | solution.py:90
  116.6 2.5 %copy.40 = f32[4,8,32,256]{3,2,1,0:T(8,128)} copy(f32[4,8,32,256]{3,1,2,0:T(8,128)} %bitcast.72) | data formatting | bytes 2097152
  122.5 4.4 %fusion.19 = f32[2,32,34,258]{3,2,1,0:T(8,128)S(1)} fusion(f32[1,32,32,256]{3,2,1,0:T(8,128)S(1)} %bitcast.59, f32[2,32,34,1]{3,2,1,0:T(8,128)} %copy.36, f32[2,32,1,256]{3,2,1,0:T(1,128)S(1)} %collective-permute-done.9, f32[1,32,32,256]{3,2,1,0:T(8,128)} %bitcast.65, f32[2,32,1,256]{3,2,1,0:T(1,128)S(1)} %collective-permute-done.8, f32[2,32,34,1]{3,2,1,0:T(8,128)} %copy.35), kind=kLoop, calls=%fused_computation.23 | loop fusion | flops 2807040 | bytes 4491264 | tf_op jit(solution)/shard_map/concatenate | solution.py:33
  129.1 3.0 %bitcast_add_fusion = f32[32,32,256]{2,1,0:T(8,128)S(1)} fusion(f32[4,8,32,256]{3,2,1,0:T(8,128)S(1)} %copy-done.9, f32[32,32,256]{2,1,0:T(8,128)S(1)} %copy-done.4, f32[32,32,256]{2,1,0:T(8,128)S(1)} %copy-done.6, f32[32,34,258]{2,1,0:T(8,128)S(1)} %get-tuple-element.67, f32[32,32,256]{2,1,0:T(8,128)S(1)} %convert_select_fusion, ...), kind=kLoop, calls=%fused_computation.47 | loop fusion | flops 8126464 | bytes 18874368 | tf_op jit(solution)/shard_map/add | solution.py:96
  132.2 15.1 %all_to_all.14 = f32[2,32,16,256]{3,2,1,0:T(8,128)S(1)} all-to-all(f32[2,32,16,256]{3,2,1,0:T(8,128)S(1)} %pad_maximum_fusion.6), channel_id=1, replica_groups=mesh['cap'=4,'lat'=4,'rad'=2] {'rad'}, dimensions={0} | all-to-all | bytes 2097152 | tf_op jit(solution)/shard_map/all_to_all | solution.py:17
  (83 shorter events, 53.1 us)
Async XLA Ops:
  0.0 147.9 %copy-start = (f32[64,64]{1,0:T(8,128)S(1)}, f32[64,64]{1,0:T(8,128)}, u32[]{:S(2)}) copy-start(f32[64,64]{1,0:T(8,128)} %param.16) | copy-start | bytes 49156
  0.0 1.9 %copy-start.1 = (f32[32,32,256]{2,1,0:T(8,128)S(1)}, f32[32,32,256]{2,1,0:T(8,128)}, u32[]{:S(2)}) copy-start(f32[32,32,256]{2,1,0:T(8,128)} %param.11) | copy-start | bytes 3145732
  2.1 5.4 %collective-permute-start = (f32[2,32,1,256]{3,2,1,0:T(1,128)S(1)}, f32[2,32,1,256]{3,2,1,0:T(1,128)S(1)}, u32[]{:S(2)}, u32[]{:S(2)}) collective-permute-start(f32[2,32,1,256]{3,2,1,0:T(1,128)S(1)} %get-tuple-element.62), channel_id=1, source_target_pairs={{0,8},{8,16},{16,24},{1,9},{9,17},{17,25},{2,10},{10,18},{18,26},{... | collective-permute-start | bytes 196616 | tf_op jit(solution)/shard_map/ppermute | solution.py:31
  6.1 5.0 %collective-permute-start.1 = (f32[2,32,1,256]{3,2,1,0:T(1,128)S(1)}, f32[2,32,1,256]{3,2,1,0:T(1,128)S(1)}, u32[]{:S(2)}, u32[]{:S(2)}) collective-permute-start(f32[2,32,1,256]{3,2,1,0:T(1,128)S(1)} %get-tuple-element.84), channel_id=1, source_target_pairs={{8,0},{16,8},{24,16},{9,1},{17,9},{25,17},{10,2},{18,10},{26,18},{... | collective-permute-start | bytes 196616 | tf_op jit(solution)/shard_map/ppermute | solution.py:32
  15.3 8.9 %collective-permute-start.2 = (f32[2,32,34,1]{2,1,3,0:T(8,128)S(1)}, f32[2,32,34,1]{2,1,3,0:T(8,128)S(1)}, u32[]{:S(2)}, u32[]{:S(2)}) collective-permute-start(f32[2,32,34,1]{2,1,3,0:T(8,128)S(1)} %copy.25), channel_id=1, source_target_pairs={{0,2},{2,4},{4,6},{1,3},{3,5},{5,7},{8,10},{10,12},{12,14},{9,11},... | collective-permute-start | bytes 26120 | tf_op jit(solution)/shard_map/ppermute | solution.py:31
  22.3 5.2 %collective-permute-start.3 = (f32[2,32,34,1]{2,1,3,0:T(8,128)S(1)}, f32[2,32,34,1]{2,1,3,0:T(8,128)S(1)}, u32[]{:S(2)}, u32[]{:S(2)}) collective-permute-start(f32[2,32,34,1]{2,1,3,0:T(8,128)S(1)} %copy.26), channel_id=1, source_target_pairs={{2,0},{4,2},{6,4},{3,1},{5,3},{7,5},{10,8},{12,10},{14,12},{11,9},... | collective-permute-start | bytes 26120 | tf_op jit(solution)/shard_map/ppermute | solution.py:32
  33.4 1.2 copy-start.2
  34.7 8.2 %copy-start.11 = (bf16[32,2048]{1,0:T(8,128)(2,1)S(1)}, bf16[32,2048]{1,0:T(8,128)(2,1)}, u32[]{:S(2)}) copy-start(bf16[32,2048]{1,0:T(8,128)(2,1)} %param.17) | copy-start | bytes 393220
  38.4 8.5 %collective-permute-start.4 = (f32[2,32,1,256]{3,2,1,0:T(1,128)}, f32[2,32,1,256]{3,2,1,0:T(1,128)S(1)}, u32[]{:S(2)}, u32[]{:S(2)}) collective-permute-start(f32[2,32,1,256]{3,2,1,0:T(1,128)} %get-tuple-element.82), channel_id=1, source_target_pairs={{0,8},{8,16},{16,24},{1,9},{9,17},{17,25},{2,10},{10,18},{18,26},{... | collective-permute-start | bytes 196616 | tf_op jit(solution)/shard_map/ppermute | solution.py:31
  41.6 5.3 %collective-permute-start.5 = (f32[2,32,1,256]{3,2,1,0:T(1,128)S(1)}, f32[2,32,1,256]{3,2,1,0:T(1,128)S(1)}, u32[]{:S(2)}, u32[]{:S(2)}) collective-permute-start(f32[2,32,1,256]{3,2,1,0:T(1,128)S(1)} %get-tuple-element.83), channel_id=1, source_target_pairs={{8,0},{16,8},{24,16},{9,1},{17,9},{25,17},{10,2},{18,10},{26,18},{... | collective-permute-start | bytes 196616 | tf_op jit(solution)/shard_map/ppermute | solution.py:32
  43.5 51.8 %all-to-all-start = ((bf16[32,4,512]{2,0,1:T(8,128)(2,1)}), bf16[32,4,512]{2,0,1:T(8,128)(2,1)S(1)}, u32[]{:S(2)}, u32[]{:S(2)}) async-start(bf16[32,4,512]{2,0,1:T(8,128)(2,1)} %bitcast.48), calls=%async_computation | async-start | bytes 262144 | tf_op jit(solution)/shard_map/all_to_all | solution.py:74
  50.4 9.0 %copy-start.13 = (s32[4]{0:T(128)S(1)}, s32[4]{0:T(128)}, u32[]{:S(2)}) copy-start(s32[4]{0:T(128)} %param.19) | copy-start | bytes 52
  52.2 7.2 %collective-permute-start.6 = (f32[2,32,34,1]{2,1,3,0:T(8,128)S(1)}, f32[2,32,34,1]{2,1,3,0:T(8,128)S(1)}, u32[]{:S(2)}, u32[]{:S(2)}) collective-permute-start(f32[2,32,34,1]{2,1,3,0:T(8,128)S(1)} %copy.29), channel_id=1, source_target_pairs={{0,2},{2,4},{4,6},{1,3},{3,5},{5,7},{8,10},{10,12},{12,14},{9,11},... | collective-permute-start | bytes 26120 | tf_op jit(solution)/shard_map/ppermute | solution.py:31
  57.2 5.3 %collective-permute-start.7 = (f32[2,32,34,1]{2,1,3,0:T(8,128)S(1)}, f32[2,32,34,1]{2,1,3,0:T(8,128)}, u32[]{:S(2)}, u32[]{:S(2)}) collective-permute-start(f32[2,32,34,1]{2,1,3,0:T(8,128)S(1)} %copy.30), channel_id=1, source_target_pairs={{2,0},{4,2},{6,4},{3,1},{5,3},{7,5},{10,8},{12,10},{14,12},{11,9},... | collective-permute-start | bytes 26120 | tf_op jit(solution)/shard_map/ppermute | solution.py:32
  69.4 1.5 %copy-start.8 = (f32[32,32,256]{2,1,0:T(8,128)S(1)}, f32[32,32,256]{2,1,0:T(8,128)}, u32[]{:S(2)}) copy-start(f32[32,32,256]{2,1,0:T(8,128)} %copy-done.7) | copy-start | bytes 3145732
  70.9 7.8 %copy-start.12 = (s32[2048]{0:T(1024)S(1)}, s32[2048]{0:T(1024)}, u32[]{:S(2)}) copy-start(s32[2048]{0:T(1024)} %param.18) | copy-start | bytes 24580
  73.9 4.8 %collective-permute-start.8 = (f32[2,32,1,256]{3,2,1,0:T(1,128)S(1)}, f32[2,32,1,256]{3,2,1,0:T(1,128)S(1)}, u32[]{:S(2)}, u32[]{:S(2)}) collective-permute-start(f32[2,32,1,256]{3,2,1,0:T(1,128)S(1)} %get-tuple-element.80), channel_id=1, source_target_pairs={{0,8},{8,16},{16,24},{1,9},{9,17},{17,25},{2,10},{10,18},{18,26},{... | collective-permute-start | bytes 196616 | tf_op jit(solution)/shard_map/ppermute | solution.py:31
  77.4 5.0 %collective-permute-start.9 = (f32[2,32,1,256]{3,2,1,0:T(1,128)S(1)}, f32[2,32,1,256]{3,2,1,0:T(1,128)S(1)}, u32[]{:S(2)}, u32[]{:S(2)}) collective-permute-start(f32[2,32,1,256]{3,2,1,0:T(1,128)S(1)} %get-tuple-element.81), channel_id=1, source_target_pairs={{8,0},{16,8},{24,16},{9,1},{17,9},{25,17},{10,2},{18,10},{26,18},{... | collective-permute-start | bytes 196616 | tf_op jit(solution)/shard_map/ppermute | solution.py:32
  87.7 31.5 %collective-permute-start.10 = (f32[2,32,34,1]{2,1,3,0:T(8,128)S(1)}, f32[2,32,34,1]{2,1,3,0:T(8,128)S(1)}, u32[]{:S(2)}, u32[]{:S(2)}) collective-permute-start(f32[2,32,34,1]{2,1,3,0:T(8,128)S(1)} %copy.33), channel_id=1, source_target_pairs={{0,2},{2,4},{4,6},{1,3},{3,5},{5,7},{8,10},{10,12},{12,14},{9,11},... | collective-permute-start | bytes 26120 | tf_op jit(solution)/shard_map/ppermute | solution.py:31
  93.1 27.7 %collective-permute-start.11 = (f32[2,32,34,1]{2,1,3,0:T(8,128)S(1)}, f32[2,32,34,1]{2,1,3,0:T(8,128)S(1)}, u32[]{:S(2)}, u32[]{:S(2)}) collective-permute-start(f32[2,32,34,1]{2,1,3,0:T(8,128)S(1)} %copy.34), channel_id=1, source_target_pairs={{2,0},{4,2},{6,4},{3,1},{5,3},{7,5},{10,8},{12,10},{14,12},{11,9},... | collective-permute-start | bytes 26120 | tf_op jit(solution)/shard_map/ppermute | solution.py:32
  126.9 1.2 copy-start.4
  126.9 1.5 %copy-start.6 = (f32[32,32,256]{2,1,0:T(8,128)S(1)}, f32[32,32,256]{2,1,0:T(8,128)}, u32[]{:S(2)}) copy-start(f32[32,32,256]{2,1,0:T(8,128)} %copy-done.5) | copy-start | bytes 3145732
  126.9 1.8 %copy-start.9 = (f32[4,8,32,256]{3,2,1,0:T(8,128)S(1)}, f32[4,8,32,256]{3,2,1,0:T(8,128)}, u32[]{:S(2)}) copy-start(f32[4,8,32,256]{3,2,1,0:T(8,128)} %copy.40) | copy-start | bytes 3145732
  126.9 2.1 %copy-start.10 = (bf16[2,32,32,256]{3,2,1,0:T(8,128)(2,1)S(1)}, bf16[2,32,32,256]{3,2,1,0:T(8,128)(2,1)}, u32[]{:S(2)}) copy-start(bf16[2,32,32,256]{3,2,1,0:T(8,128)(2,1)} %param.12) | copy-start | bytes 3145732
  (3 other events, 3.2 us)
